TPU v7x, 512 devices: a whole 4x4x16 slice. The times are simulated.
512 devices in a mesh: ctx: 64 (over z, x_hi, core), head: 8 (over y, x_lo).
Axes of the slice: x: 4 (x_hi: 2, x_lo: 2; x = x_hi * 2 + x_lo), y: 4, z: 16, core: 2. Of those that a mesh axis runs over, the one named last changes fastest.
Arguments:
- tokens: bfloat16 [8192, 4096], P('ctx'), may hold values from -6 to 6
- norm_gain: float32 [4096], replicated, may hold values from 0.25 to 1.75
- w_query: bfloat16 [4096, 4096], P('ctx', 'head'), may hold values from -0.09375 to 0.09375
- w_key: bfloat16 [4096, 1024], P('ctx', 'head'), may hold values from -0.09375 to 0.09375
- w_value: bfloat16 [4096, 1024], P('ctx', 'head'), may hold values from -0.09375 to 0.09375
- w_out: bfloat16 [4096, 4096], P('head', 'ctx'), may hold values from -0.09375 to 0.09375
- row_map: int32 [8192], P('ctx'), may hold values from 0 to 8191, as said below
- doc_lengths: int32 [32], replicated, may hold values from 1 to 2048, 8192 in all
- doc_labels: int32 [32], replicated, may hold values from 0 to 1, as said below
Outputs:
- residual_out: bfloat16 [8192, 4096], P('ctx', 'head')
- refusal_direction: float32 [4096], P('head')
Inputs may be any that keep to these rules, and one draw needn't show every extreme that they name: `row_map`: the rows of ctx index c are two runs of 64 consecutive positions, run b(c) and run 2 * 64 - 1 - b(c) of the pack, b a permutation drawn from the seed; every position appears once. `doc_labels`: at least one prompt of each class.
All inputs are finite; a program needn't handle non-finite values.
Results may differ from a plain program's by a relative error of at most 0.008.
Values may be sent and summed in bfloat16 or wider, within the bound.
No kernel may reach another device: no remote copies, remote signals or barrier semaphores. Data moves between devices by JAX's collectives and lax.ppermute only.
A program may use at most 64 MiB of HBM per device.

v0:
```python
import math
import jax
import jax.numpy as jnp
from jax import lax
from jax.sharding import PartitionSpec as P

HEADS = 32
KV_HEADS = 8
HEAD_DIM = 128
ROPE_BASE = 500000.0
NEG_FILL = -1e30
BLOCK_KEYS = 512


def doc_layout(row_map, doc_lengths):
    doc_ends = jnp.cumsum(doc_lengths)
    doc_starts = doc_ends - doc_lengths
    doc_index = jnp.sum((row_map[:, None] >= doc_ends[None, :]).astype(jnp.int32), 1)
    member = doc_index[:, None] == jnp.arange(doc_ends.shape[0], dtype=jnp.int32)[None, :]
    in_doc = row_map - jnp.sum(jnp.where(member, doc_starts[None, :], 0), 1)
    return (doc_index, in_doc, doc_ends)


def rotate(values, in_doc):
    head_dim = values.shape[-1]
    half_dim = head_dim // 2
    inv_freq = jnp.exp(
        jnp.arange(half_dim).astype(jnp.float32) * (-2.0 * math.log(ROPE_BASE) / head_dim)
    )
    angles = in_doc.astype(jnp.float32)[:, None] * inv_freq[None, :]
    shape_out = (angles.shape[0],) + (1,) * (values.ndim - 2) + (half_dim,)
    cosine = jnp.cos(angles).reshape(shape_out)
    sine_val = jnp.sin(angles).reshape(shape_out)
    front_half = values[..., :half_dim]
    back_half = values[..., half_dim:]
    return jnp.concatenate(
        [front_half * cosine - back_half * sine_val, back_half * cosine + front_half * sine_val], -1
    )


def rms_norm(tokens, norm_gain):
    wide_tokens = tokens.astype(jnp.float32)
    row_scale = lax.rsqrt(jnp.mean(wide_tokens * wide_tokens, -1, keepdims=True) + 1e-05)
    return (wide_tokens * row_scale * norm_gain).astype(jnp.bfloat16)


def attend_keys(carried, key_block_set, queries, query_pos, query_doc, doc_ends):
    key_block, value_block, key_pos = key_block_set
    key_doc = jnp.sum((key_pos[:, None] >= doc_ends[None, :]).astype(jnp.int32), 1)
    allowed = (key_doc[None, :] == query_doc[:, None]) & (key_pos[None, :] <= query_pos[:, None])
    scale_factor = queries.shape[-1] ** (-0.5)
    running_max, running_sum, weighted = carried
    scores = (
        jnp.einsum("qgjd,kgd->gjqk", queries, key_block, preferred_element_type=jnp.float32)
        * scale_factor
    )
    scores = jnp.where(allowed[None, None], scores, NEG_FILL)
    new_max = jnp.maximum(running_max, jnp.max(scores, -1))
    weights = jnp.where(allowed[None, None], jnp.exp(scores - new_max[..., None]), 0.0)
    rescale = jnp.exp(running_max - new_max)
    new_sum = running_sum * rescale + jnp.sum(weights, -1)
    new_weighted = weighted * rescale[..., None] + jnp.einsum(
        "gjqk,kgd->gjqd",
        weights.astype(jnp.bfloat16),
        value_block,
        preferred_element_type=jnp.float32,
    )
    return (new_max, new_sum, new_weighted)


def make_fold(queries, query_pos, query_doc, doc_ends):

    def fold_keys(carried, pieces, offset):
        key_rows = pieces[0].shape[0]
        step_count = key_rows // BLOCK_KEYS
        stacked = tuple(
            (member.reshape((step_count, BLOCK_KEYS) + member.shape[1:]) for member in pieces)
        )

        def scan_step(softmax_state, key_block_set):
            return (
                attend_keys(softmax_state, key_block_set, queries, query_pos, query_doc, doc_ends),
                None,
            )

        final_state, unused = lax.scan(scan_step, carried, stacked)
        return final_state

    return fold_keys


def local(tokens, norm_gain, w_query, w_key, w_value, w_out, row_map, doc_lengths, doc_labels):
    tok_rows = tokens.shape[0]
    kv_local = w_key.shape[1] // HEAD_DIM
    group_size = HEADS // KV_HEADS
    normed = rms_norm(tokens, norm_gain)
    weight_pieces = (
        lax.all_gather(w_query, "ctx", axis=0, tiled=True),
        lax.all_gather(w_key, "ctx", axis=0, tiled=True),
        lax.all_gather(w_value, "ctx", axis=0, tiled=True),
    )
    queries, key_proj, value_proj = tuple(
        (
            jnp.dot(normed, weight_piece, preferred_element_type=jnp.float32)
            for weight_piece in weight_pieces
        )
    )
    doc_index, in_doc, doc_ends = doc_layout(row_map, doc_lengths)
    queries = rotate(queries.reshape(tok_rows, kv_local, group_size, HEAD_DIM), in_doc).astype(
        jnp.bfloat16
    )
    key_proj = rotate(key_proj.reshape(tok_rows, kv_local, HEAD_DIM), in_doc).astype(jnp.bfloat16)
    value_proj = value_proj.reshape(tok_rows, kv_local, HEAD_DIM).astype(jnp.bfloat16)
    initial = (
        jnp.full((kv_local, group_size, tok_rows), NEG_FILL, jnp.float32),
        jnp.zeros((kv_local, group_size, tok_rows), jnp.float32),
        jnp.zeros((kv_local, group_size, tok_rows, HEAD_DIM), jnp.float32),
    )
    fold_keys = make_fold(queries, row_map, doc_index, doc_ends)
    softmax_state = fold_keys(
        initial,
        (
            lax.all_gather(key_proj, "ctx", axis=0, tiled=True),
            lax.all_gather(value_proj, "ctx", axis=0, tiled=True),
            lax.all_gather(row_map, "ctx", axis=0, tiled=True),
        ),
        jnp.int32(0),
    )
    running_max, running_sum, weighted = softmax_state
    attended = weighted / running_sum[..., None]
    attended = (
        jnp.transpose(attended, (2, 0, 1, 3))
        .reshape(tok_rows, kv_local * group_size * HEAD_DIM)
        .astype(jnp.bfloat16)
    )
    partial_out = jnp.dot(
        attended,
        lax.all_gather(w_out, "ctx", axis=1, tiled=True),
        preferred_element_type=jnp.float32,
    )
    head_share = lax.psum_scatter(
        partial_out.astype(jnp.bfloat16), "head", scatter_dimension=1, tiled=True
    ).astype(jnp.float32)
    col_width = head_share.shape[1]
    own_cols = lax.dynamic_slice_in_dim(tokens, lax.axis_index("head") * col_width, col_width, 1)
    residual_out = (own_cols.astype(jnp.float32) + head_share).astype(jnp.bfloat16)
    is_last = row_map[:, None] == (doc_ends - 1)[None, :]
    label_f = doc_labels.astype(jnp.float32)
    harmful = jnp.sum(label_f)
    harmless = doc_labels.shape[0] - jnp.sum(label_f)
    stream = residual_out.astype(jnp.float32)
    harm_rows = jnp.sum(jnp.where(is_last, label_f[None, :], 0.0), 1)
    safe_rows = jnp.sum(jnp.where(is_last, (1.0 - label_f)[None, :], 0.0), 1)
    harm_sum, safe_sum = lax.psum(
        (jnp.sum(harm_rows[:, None] * stream, 0), jnp.sum(safe_rows[:, None] * stream, 0)), "ctx"
    )
    refusal_direction = harm_sum / harmful - safe_sum / harmless
    return (residual_out, refusal_direction)


def solution(mesh):
    placed = (
        P("ctx", None),
        P(),
        P("ctx", "head"),
        P("ctx", "head"),
        P("ctx", "head"),
        P("head", "ctx"),
        P("ctx"),
        P(),
        P(),
    )
    return jax.shard_map(
        local, mesh=mesh, in_specs=placed, out_specs=(P("ctx", "head"), P("head")), check_vma=False
    )
```

profile of v0, /device:TPU:1, one launch (start us, length us, event | category | flops | bytes accessed | tf_op | source)
XLA Modules:
  0.0 1057.2 jit_solution(1660407853010582978)
XLA Ops:
  11.1 1.5 fusion.19
  13.3 143.4 %all-gather.9.cloned.1.call-done = bf16[4096,128]{1,0:T(8,128)(2,1)} async-done(((bf16[64,128]{1,0:T(8,128)(2,1)}), bf16[4096,128]{1,0:T(8,128)(2,1)}) %all-gather.9.cloned.1.call-update) | async-done | bytes 1048592 | tf_op jit(solution)/shard_map/all_gather | solution.py:99
  156.8 2.2 convolution_bitcast_fusion.1
  160.4 134.9 %all-gather.15.cloned.1.call-done = bf16[4096,128]{1,0:T(8,128)(2,1)} async-done(((bf16[64,128]{1,0:T(8,128)(2,1)}), bf16[4096,128]{1,0:T(8,128)(2,1)}) %all-gather.15.cloned.1.call-update) | async-done | bytes 1048592 | tf_op jit(solution)/shard_map/all_gather | solution.py:100
  295.4 2.3 convolution_convert_fusion.1
  298.7 74.1 %all-gather.1 = s32[64,1,128]{2,1,0:T(1,128)S(1)} all-gather(s32[1,1,128]{2,1,0:T(1,128)S(1)} %bitcast.82), channel_id=1, replica_groups=mesh['ctx'=64,'head'=8] {'ctx'}, dimensions={0}, use_global_device_ids=true | all-gather | bytes 33280 | tf_op jit(solution)/shard_map/all_gather | solution.py:125
  374.1 57.8 %all-gather.11.cloned.1.call-done = bf16[8192,1,128]{0,2,1:T(8,128)(2,1)} async-done(((bf16[128,1,128]{0,2,1:T(8,128)(2,1)}), bf16[8192,1,128]{0,2,1:T(8,128)(2,1)}) %all-gather.11.cloned.1.call-update) | async-done | bytes 2097168 | tf_op jit(solution)/shard_map/all_gather | solution.py:123
  431.9 4.1 copy.39
  436.0 144.2 %all-gather.13.cloned.1.call-done = bf16[4096,512]{1,0:T(8,128)(2,1)} async-done(((bf16[64,512]{1,0:T(8,128)(2,1)}), bf16[4096,512]{1,0:T(8,128)(2,1)}) %all-gather.13.cloned.1.call-update) | async-done | bytes 4194320 | tf_op jit(solution)/shard_map/all_gather | solution.py:98
  580.1 2.9 fusion.35
  583.6 138.0 %all-gather.19.cloned.1.call-done = bf16[8192,128]{1,0:T(8,128)(2,1)} async-done(((bf16[128,128]{1,0:T(8,128)(2,1)}), bf16[8192,128]{1,0:T(8,128)(2,1)}) %all-gather.19.cloned.1.call-update) | async-done | bytes 2097168 | tf_op jit(solution)/shard_map/all_gather | solution.py:124
  721.6 50.8 %while.15 = (s32[]{:T(128)}, f32[1,4,128]{2,1,0:T(4,128)S(1)}, f32[1,4,128]{2,1,0:T(4,128)S(1)}, f32[1,4,128,128]{3,2,1,0:T(8,128)S(1)}, s32[16,512]{1,0:T(8,128...) while((s32[]{:T(128)}, f32[1,4,128]{2,1,0:T(4,128)S(1)}, ...), condition=%wide.region_8.9_spmd.clone, body=%wide.region_4.8_spmd.clone.sunk | while | flops 137021952 | bytes 4372749 | solution.py:86
  723.1 1.3 fusion.57
  725.0 1.2 fusion.54
  726.3 1.4 fusion.57
  728.2 1.2 fusion.54
  729.5 1.4 fusion.57
  731.4 1.2 fusion.54
  732.6 1.4 fusion.57
  734.6 1.2 fusion.54
  735.8 1.4 fusion.57
  737.7 1.2 fusion.54
  739.0 1.4 fusion.57
  740.9 1.2 fusion.54
  742.2 1.4 fusion.57
  744.1 1.2 fusion.54
  745.3 1.4 fusion.57
  747.3 1.2 fusion.54
  748.5 1.4 fusion.57
  750.4 1.2 fusion.54
  751.7 1.4 fusion.57
  753.6 1.2 fusion.54
  754.9 1.4 fusion.57
  756.8 1.2 fusion.54
  758.0 1.4 fusion.57
  760.0 1.2 fusion.54
  761.2 1.4 fusion.57
  763.1 1.2 fusion.54
  764.4 1.4 fusion.57
  766.3 1.2 fusion.54
  767.6 1.4 fusion.57
  769.5 1.2 fusion.54
  770.7 1.3 fusion.57
  772.5 97.7 %all-gather.17.cloned.1.call-done = bf16[512,4096]{0,1:T(8,128)(2,1)} async-done(((bf16[512,64]{0,1:T(8,128)(2,1)}), bf16[512,4096]{0,1:T(8,128)(2,1)}) %all-gather.17.cloned.1.call-update) | async-done | bytes 4194320 | tf_op jit(solution)/shard_map/all_gather | solution.py:138
  870.2 4.7 convolution_convert_fusion
  876.2 37.1 %reduce-scatter.2.cloned.1.call-done = bf16[128,512]{1,0:T(8,128)(2,1)} async-done(((bf16[128,4096]{1,0:T(8,128)(2,1)}), bf16[128,512]{1,0:T(8,128)(2,1)}) %reduce-scatter.2.cloned.1.call-update) | async-done | bytes 131088 | tf_op jit(solution)/shard_map/reduce_scatter | solution.py:141
  913.3 1.6 fusion.22
  914.9 134.3 %all-reduce = (f32[512]{0:T(512)S(1)}, f32[512]{0:T(512)S(1)}) all-reduce(f32[512]{0:T(512)S(1)} %get-tuple-element.143, f32[512]{0:T(512)S(1)} %get-tuple-element.142), channel_id=1, replica_groups=mesh['ctx'=64,'head'=8] {'ctx'}, use_global_device_ids=true, to_apply=%region_16.17 | all-reduce | flops 1024 | bytes 8192 | tf_op jit(solution)/shard_map/psum | solution.py:154
  (163 shorter events, 20.6 us)
Async XLA Ops:
  7.2 288.2 %copy-start = (bf16[128,4096]{1,0:T(8,128)(2,1)S(1)}, bf16[128,4096]{1,0:T(8,128)(2,1)}, u32[]{:S(2)}) copy-start(bf16[128,4096]{1,0:T(8,128)(2,1)} %param.11) | copy-start | bytes 3145732
  7.2 288.2 %copy-start.2 = (f32[4096]{0:T(1024)S(1)}, f32[4096]{0:T(1024)}, u32[]{:S(2)}) copy-start(f32[4096]{0:T(1024)} %param.12) | copy-start | bytes 49156
  7.2 149.6 %all-gather.9.cloned.1.call-start = ((), (), s32[]{:S(2)}) async-start(), calls=%async_computation.1 | async-start | bytes 1064960 | tf_op jit(solution)/shard_map/all_gather | solution.py:99
  7.9 287.5 %all-gather.15.cloned.1.call-start = ((), (), s32[]{:S(2)}) async-start(), calls=%async_computation.4 | async-start | bytes 1064960 | tf_op jit(solution)/shard_map/all_gather | solution.py:100
  8.7 423.2 %all-gather.11.cloned.1.call-start = ((), (), s32[]{:S(2)}) async-start(), calls=%async_computation.2 | async-start | bytes 2129920 | tf_op jit(solution)/shard_map/all_gather | solution.py:123
  158.9 139.8 %copy-start.1 = (s32[128]{0:T(128)S(1)}, s32[128]{0:T(128)}, u32[]{:S(2)}) copy-start(s32[128]{0:T(128)} %param.17) | copy-start | bytes 1540
  159.8 420.3 %all-gather.13.cloned.1.call-start = ((), (), s32[]{:S(2)}) async-start(), calls=%async_computation.3 | async-start | bytes 4259840 | tf_op jit(solution)/shard_map/all_gather | solution.py:98
  160.4 561.2 %all-gather.19.cloned.1.call-start = ((), (), s32[]{:S(2)}) async-start(), calls=%async_computation.7 | async-start | bytes 2129920 | tf_op jit(solution)/shard_map/all_gather | solution.py:124
  297.7 572.5 %all-gather.17.cloned.1.call-start = ((), (), s32[]{:S(2)}) async-start(), calls=%async_computation.5 | async-start | bytes 4259840 | tf_op jit(solution)/shard_map/all_gather | solution.py:138
  298.3 615.0 %reduce-scatter.2.cloned.1.call-start = ((), (), s32[]{:S(2)}) async-start(), calls=%async_computation.6 | async-start | bytes 1179648 | tf_op jit(solution)/shard_map/reduce_scatter | solution.py:141
  870.2 4.7 copy-start.3
Sparse Core Ops, SparseCore 0:
  11.3 145.4 all-gather.8
  160.1 135.2 all-gather.14
  299.0 132.8 all-gather.10
  435.0 145.0 all-gather.12
  583.3 138.2 all-gather.18
  724.7 145.4 all-gather.16
  875.0 38.2 reduce-scatter.1
where the time goes:
time: 1060 us
  waiting for transfers between devices  756 us (71%)
  blocking collectives  208 us (20%)
  matrix products  53.2 us (5%)
  other arithmetic  17.8 us (2%)
  between operations  14.9 us (1%)
    all_gather x1, waiting for transfers between devices, local(): lax.all_gather(w_query, 'ctx', axis=0, tiled=True)  144 us
    all_gather x1, waiting for transfers between devices, local(): lax.all_gather(w_key, 'ctx', axis=0, tiled=True)  143 us
    all_gather x1, waiting for transfers between devices, local(): lax.all_gather(value_proj, 'ctx', axis=0, tiled=True)  138 us
    all_gather x1, waiting for transfers between devices, local(): lax.all_gather(w_value, 'ctx', axis=0, tiled=True)  135 us
    psum x1, blocking collectives, local(): lax.psum((jnp.sum(harm_rows[:, None] * stream, 0), jnp.sum(safe_rows[:, N...  134 us
    all_gather x1, waiting for transfers between devices, local(): lax.all_gather(w_out, 'ctx', axis=1, tiled=True)  97.7 us
    all_gather x1, blocking collectives, local(): lax.all_gather(row_map, 'ctx', axis=0, tiled=True)  74.1 us
    all_gather x1, waiting for transfers between devices, local(): lax.all_gather(key_proj, 'ctx', axis=0, tiled=True)  57.8 us
  transfers between devices with their start and end apart: 7, of which 7 were waited for; matrix products, arithmetic and copies ran while one was open for 7% of the time, Pallas kernels for 0%

commit v1 on v0

--- a/solution.py
+++ b/solution.py
@@ -121,7 +121,9 @@
         initial,
         (
             lax.all_gather(key_proj, "ctx", axis=0, tiled=True),
-            lax.all_gather(value_proj, "ctx", axis=0, tiled=True),
+            jnp.concatenate(
+                lax.all_to_all(jnp.stack([value_proj] * lax.axis_size("ctx")), "ctx", 0, 0), axis=0
+            ),
             lax.all_gather(row_map, "ctx", axis=0, tiled=True),
         ),
         jnp.int32(0),

time: 1060 us -> 952 us (0.90)
  waiting for transfers between devices: 756 us -> 553 us
  blocking collectives: 208 us -> 293 us
    all_gather x1 -> x0, waiting for transfers between devices: 138 us -> none  [local(): lax.all_gather(value_proj, 'ctx', axis=0, tiled=True)]
    all_gather x1, blocking collectives: 74.1 us -> 159 us  [local(): lax.all_gather(row_map, 'ctx', axis=0, tiled=True)]
    all_gather x1, waiting for transfers between devices: 57.8 us -> 0.02 us  [local(): lax.all_gather(key_proj, 'ctx', axis=0, tiled=True)]
  transfers between devices with their start and end apart: 7 -> 7, of which waited for: 7 -> 5; matrix products, arithmetic and copies ran while one was open for 7% -> 7% of each run, Pallas kernels for 0% -> 0%
where the time goes in v1:
time: 952 us; the launch traced here: 951 us
  waiting for transfers between devices  553 us (58%)
  blocking collectives  293 us (31%)
  matrix products  52.8 us (6%)
  other arithmetic  17.8 us (2%)
  between operations  14.9 us (2%)
  starting transfers between devices  10.2 us (1%)
    all_gather x1, blocking collectives, local(): lax.all_gather(row_map, 'ctx', axis=0, tiled=True)  159 us
    all_gather x1, waiting for transfers between devices, local(): lax.all_gather(w_key, 'ctx', axis=0, tiled=True)  143 us
    all_gather x1, waiting for transfers between devices, local(): lax.all_gather(w_query, 'ctx', axis=0, tiled=True)  141 us
    all_gather x1, waiting for transfers between devices, local(): lax.all_gather(w_value, 'ctx', axis=0, tiled=True)  135 us
    psum x1, blocking collectives, local(): lax.psum((jnp.sum(harm_rows[:, None] * stream, 0), jnp.sum(safe_rows[:, N...  134 us
    all_gather x1, waiting for transfers between devices, local(): lax.all_gather(w_out, 'ctx', axis=1, tiled=True)  94.2 us
    reduce_scatter x1, waiting for transfers between devices, local(): lax.psum_scatter(partial_out.astype(jnp.bfloat16), 'head', scatter_dimens...  37.1 us
    dot_general x16, matrix products, attend_keys(): jnp.einsum('gjqk,kgd->gjqd', weights.astype(jnp.bfloat16), value_block, p...  21.7 us
  transfers between devices with their start and end apart: 7, of which 5 were waited for; matrix products, arithmetic and copies ran while one was open for 7% of the time, Pallas kernels for 0%

profile of v1, /device:TPU:1, one launch (start us, length us, event | category | flops | bytes accessed | tf_op | source)
XLA Modules:
  0.0 950.9 jit_solution(5463650271351038007)
XLA Ops:
  11.1 1.5 fusion.19
  13.3 143.4 %all-gather.7.cloned.1.call-done = bf16[4096,128]{1,0:T(8,128)(2,1)} async-done(((bf16[64,128]{1,0:T(8,128)(2,1)}), bf16[4096,128]{1,0:T(8,128)(2,1)}) %all-gather.7.cloned.1.call-update) | async-done | bytes 1048592 | tf_op jit(solution)/shard_map/all_gather | solution.py:99
  156.8 2.2 convolution_bitcast_fusion.1
  160.4 135.0 %all-gather.13.cloned.1.call-done = bf16[4096,128]{1,0:T(8,128)(2,1)} async-done(((bf16[64,128]{1,0:T(8,128)(2,1)}), bf16[4096,128]{1,0:T(8,128)(2,1)}) %all-gather.13.cloned.1.call-update) | async-done | bytes 1048592 | tf_op jit(solution)/shard_map/all_gather | solution.py:100
  295.4 1.7 convolution_convert_fusion.1
  297.1 1.9 stack.2
  299.0 9.9 %all-to-all-start = ((bf16[64,128,1,128]{3,1,2,0:T(8,128)(2,1)}), bf16[64,128,1,128]{3,1,2,0:T(8,128)(2,1)}, u32[]{:S(2)}, u32[]{:S(2)}) async-start(bf16[64,128,1,128]{3,1,2,0:T(8,128)(2,1)} %stack.2), calls=%async_computation | async-start | bytes 4194304 | tf_op jit(solution)/shard_map/all_to_all | solution.py:125
  309.6 158.9 %all-gather = s32[64,1,128]{2,1,0:T(1,128)S(1)} all-gather(s32[1,1,128]{2,1,0:T(1,128)S(1)} %bitcast.81), channel_id=1, replica_groups=mesh['ctx'=64,'head'=8] {'ctx'}, dimensions={0}, use_global_device_ids=true | all-gather | bytes 33280 | tf_op jit(solution)/shard_map/all_gather | solution.py:127
  470.2 4.1 copy.37
  474.3 140.8 %all-gather.11.cloned.1.call-done = bf16[4096,512]{1,0:T(8,128)(2,1)} async-done(((bf16[64,512]{1,0:T(8,128)(2,1)}), bf16[4096,512]{1,0:T(8,128)(2,1)}) %all-gather.11.cloned.1.call-update) | async-done | bytes 4194320 | tf_op jit(solution)/shard_map/all_gather | solution.py:98
  615.1 2.9 fusion.35
  618.6 50.9 %while.15 = (s32[]{:T(128)}, f32[1,4,128]{2,1,0:T(4,128)S(1)}, f32[1,4,128]{2,1,0:T(4,128)S(1)}, f32[1,4,128,128]{3,2,1,0:T(8,128)S(1)}, s32[16,512]{1,0:T(8,128...) while((s32[]{:T(128)}, f32[1,4,128]{2,1,0:T(4,128)S(1)}, ...), condition=%wide.region_8.9_spmd.clone, body=%wide.region_4.8_spmd.clone.sunk | while | flops 137021952 | bytes 4372749 | solution.py:86
  618.9 1.2 fusion.54
  620.2 1.4 fusion.57
  622.1 1.2 fusion.54
  623.3 1.4 fusion.57
  625.3 1.2 fusion.54
  626.5 1.4 fusion.57
  628.5 1.2 fusion.54
  629.7 1.4 fusion.57
  631.6 1.2 fusion.54
  632.9 1.4 fusion.57
  634.8 1.2 fusion.54
  636.1 1.4 fusion.57
  638.0 1.2 fusion.54
  639.2 1.4 fusion.57
  641.2 1.2 fusion.54
  642.4 1.4 fusion.57
  644.4 1.2 fusion.54
  645.6 1.4 fusion.57
  647.5 1.2 fusion.54
  648.8 1.4 fusion.57
  650.7 1.2 fusion.54
  652.0 1.4 fusion.57
  653.9 1.2 fusion.54
  655.1 1.4 fusion.57
  657.1 1.2 fusion.54
  658.3 1.4 fusion.57
  660.3 1.2 fusion.54
  661.5 1.4 fusion.57
  664.7 1.4 fusion.57
  666.6 1.2 fusion.54
  667.9 1.4 fusion.57
  669.6 94.2 %all-gather.15.cloned.1.call-done = bf16[512,4096]{0,1:T(8,128)(2,1)} async-done(((bf16[512,64]{0,1:T(8,128)(2,1)}), bf16[512,4096]{0,1:T(8,128)(2,1)}) %all-gather.15.cloned.1.call-update) | async-done | bytes 4194320 | tf_op jit(solution)/shard_map/all_gather | solution.py:140
  763.9 4.7 convolution_convert_fusion
  769.9 37.1 %reduce-scatter.2.cloned.1.call-done = bf16[128,512]{1,0:T(8,128)(2,1)} async-done(((bf16[128,4096]{1,0:T(8,128)(2,1)}), bf16[128,512]{1,0:T(8,128)(2,1)}) %reduce-scatter.2.cloned.1.call-update) | async-done | bytes 131088 | tf_op jit(solution)/shard_map/reduce_scatter | solution.py:143
  807.0 1.6 fusion.22
  808.6 134.3 %all-reduce = (f32[512]{0:T(512)S(1)}, f32[512]{0:T(512)S(1)}) all-reduce(f32[512]{0:T(512)S(1)} %get-tuple-element.143, f32[512]{0:T(512)S(1)} %get-tuple-element.142), channel_id=1, replica_groups=mesh['ctx'=64,'head'=8] {'ctx'}, use_global_device_ids=true, to_apply=%region_16.17 | all-reduce | flops 1024 | bytes 8192 | tf_op jit(solution)/shard_map/psum | solution.py:156
  (163 shorter events, 20.6 us)
Async XLA Ops:
  7.2 288.2 %copy-start = (bf16[128,4096]{1,0:T(8,128)(2,1)S(1)}, bf16[128,4096]{1,0:T(8,128)(2,1)}, u32[]{:S(2)}) copy-start(bf16[128,4096]{1,0:T(8,128)(2,1)} %param.11) | copy-start | bytes 3145732
  7.2 288.2 %copy-start.2 = (f32[4096]{0:T(1024)S(1)}, f32[4096]{0:T(1024)}, u32[]{:S(2)}) copy-start(f32[4096]{0:T(1024)} %param.12) | copy-start | bytes 49156
  7.2 149.6 %all-gather.7.cloned.1.call-start = ((), (), s32[]{:S(2)}) async-start(), calls=%async_computation.2 | async-start | bytes 1064960 | tf_op jit(solution)/shard_map/all_gather | solution.py:99
  7.9 287.5 %all-gather.13.cloned.1.call-start = ((), (), s32[]{:S(2)}) async-start(), calls=%async_computation.5 | async-start | bytes 1064960 | tf_op jit(solution)/shard_map/all_gather | solution.py:100
  8.7 461.5 %all-gather.9.cloned.1.call-start = ((), (), s32[]{:S(2)}) async-start(), calls=%async_computation.3 | async-start | bytes 2129920 | tf_op jit(solution)/shard_map/all_gather | solution.py:123
  159.8 455.3 %all-gather.11.cloned.1.call-start = ((), (), s32[]{:S(2)}) async-start(), calls=%async_computation.4 | async-start | bytes 4259840 | tf_op jit(solution)/shard_map/all_gather | solution.py:98
  299.0 10.6 %copy-start.1 = (s32[128]{0:T(128)S(1)}, s32[128]{0:T(128)}, u32[]{:S(2)}) copy-start(s32[128]{0:T(128)} %param.17) | copy-start | bytes 1540
  299.0 319.6 %all-to-all-start = ((bf16[64,128,1,128]{3,1,2,0:T(8,128)(2,1)}), bf16[64,128,1,128]{3,1,2,0:T(8,128)(2,1)}, u32[]{:S(2)}, u32[]{:S(2)}) async-start(bf16[64,128,1,128]{3,1,2,0:T(8,128)(2,1)} %stack.2), calls=%async_computation | async-start | bytes 4194304 | tf_op jit(solution)/shard_map/all_to_all | solution.py:125
  308.9 454.9 %all-gather.15.cloned.1.call-start = ((), (), s32[]{:S(2)}) async-start(), calls=%async_computation.6 | async-start | bytes 4259840 | tf_op jit(solution)/shard_map/all_gather | solution.py:140
  309.5 497.5 %reduce-scatter.2.cloned.1.call-start = ((), (), s32[]{:S(2)}) async-start(), calls=%async_computation.7 | async-start | bytes 1179648 | tf_op jit(solution)/shard_map/reduce_scatter | solution.py:143
  763.9 4.7 copy-start.3
Sparse Core Ops, SparseCore 0:
  11.3 145.4 all-gather.6
  160.1 135.2 all-gather.12
  299.0 168.1 all-gather.8
  470.3 144.8 all-gather.10
  618.3 145.5 all-gather.14
  768.7 38.2 reduce-scatter.1
